TPU v7x, 32 devices: a whole 2x2x4 slice. The times are simulated.
32 devices in a mesh: dp: 4 (over y, x), expert: 8 (over z, core).
Axes of the slice: x: 2, y: 2, z: 4, core: 2. Of those that a mesh axis runs over, the one named last changes fastest.
Arguments:
- tokens: bfloat16 [4096, 3584], P(('dp', 'expert')), may hold values from -6 to 6
- gate_probs: float32 [4096, 8], P(('dp', 'expert')), may hold values from 0.1 to 1
- expert_ids: int32 [4096, 8], P(('dp', 'expert')), may hold values from 0 to 63, all different within a row; in each aligned block of 128 rows (0 to 127, 128 to 255, ...) at most 24 rows name the same one
- cotangent: bfloat16 [4096, 3584], P(('dp', 'expert')), may hold values from -6 to 6
- w_gate: bfloat16 [8, 3584, 2048], P('expert', None, 'dp'), may hold values from -0.09375 to 0.09375
- w_up: bfloat16 [8, 3584, 2048], P('expert', None, 'dp'), may hold values from -0.09375 to 0.09375
- w_down: bfloat16 [8, 2048, 3584], P('expert', 'dp'), may hold values from -0.125 to 0.125
Outputs:
- layer_out: bfloat16 [4096, 3584], P(('dp', 'expert'))
- grad_tokens: bfloat16 [4096, 3584], P(('dp', 'expert'))
- grad_probs: float32 [4096, 8], P(('dp', 'expert'))
- grad_gate: bfloat16 [8, 3584, 2048], P('expert', None, 'dp')
- grad_up: bfloat16 [8, 3584, 2048], P('expert', None, 'dp')
- grad_down: bfloat16 [8, 2048, 3584], P('expert', 'dp')
Inputs may be any that keep to these rules, and one draw needn't show every extreme that they name: `expert_ids`: each token names 8 distinct ids. Among the 128 tokens of one device no id is named by more than 24 of them, a bound that some block reaches. Only ids below 8 belong to the window.
All inputs are finite; a program needn't handle non-finite values.
Results may differ from a plain program's by a relative error of at most 0.012.
Values may be sent and summed in bfloat16 or wider, within the bound.
No kernel may reach another device: no remote copies, remote signals or barrier semaphores. Data moves between devices by JAX's collectives and lax.ppermute only.
A program may use at most 192 MiB of HBM per device.

v0:
```python
import jax
import jax.numpy as jnp
from jax import lax
from jax.sharding import PartitionSpec as P


def slot_table(flat_ids, experts, capacity, sentinel):
    matches = (flat_ids[:, None] == jnp.arange(experts, dtype=jnp.int32)[None, :]).astype(jnp.int32)
    earlier = jnp.cumsum(matches, axis=0) - matches
    slot_pos = jnp.sum(earlier * matches, axis=1)
    target = jnp.where(flat_ids < experts, flat_ids * capacity + slot_pos, experts * capacity)
    flat_index = jnp.arange(flat_ids.shape[0], dtype=jnp.int32)
    blank_table = jnp.full((experts * capacity,), sentinel, jnp.int32)
    return blank_table.at[target].set(flat_index, mode="drop")


def contract_last(left, right):
    return lax.dot_general(
        left, right, (((1,), (1,)), ((), ())), preferred_element_type=jnp.float32
    )


def contract_first(left, right):
    return lax.dot_general(
        left, right, (((0,), (0,)), ((), ())), preferred_element_type=jnp.float32
    )


def dispatch(send_rows):
    along_expert = lax.all_to_all(send_rows, "expert", split_axis=0, concat_axis=0, tiled=True)
    return lax.all_gather(along_expert, "dp", axis=0, tiled=True)


def gather_back(partial_rows, groups):
    summed = lax.psum_scatter(partial_rows, "dp", scatter_dimension=0, tiled=True)
    return lax.all_to_all(summed, "expert", split_axis=0, concat_axis=0, tiled=True)


def expert_forward(rows_x, gate_w, up_w, down_w):
    gate_pre = jnp.dot(rows_x, gate_w, preferred_element_type=jnp.float32)
    up_pre = jnp.dot(rows_x, up_w, preferred_element_type=jnp.float32)
    hidden = (gate_pre * jax.nn.sigmoid(gate_pre) * up_pre).astype(jnp.bfloat16)
    part_out = jnp.dot(hidden, down_w, preferred_element_type=jnp.float32).astype(jnp.bfloat16)
    return lax.optimization_barrier((part_out, hidden, gate_pre, up_pre))


def expert_backward(rows_c, gate_pre, up_pre, gate_w, up_w, down_w):
    sigmoid_g = jax.nn.sigmoid(gate_pre)
    activated = gate_pre * sigmoid_g
    grad_hidden = contract_last(rows_c, down_w)
    grad_upin = (grad_hidden * activated).astype(jnp.bfloat16)
    grad_gatein = (grad_hidden * up_pre * sigmoid_g * (1.0 + gate_pre * (1.0 - sigmoid_g))).astype(
        jnp.bfloat16
    )
    part_dx = (contract_last(grad_gatein, gate_w) + contract_last(grad_upin, up_w)).astype(
        jnp.bfloat16
    )
    return (part_dx, grad_gatein, grad_upin)


def join_slots(chunks, experts, model_width):
    parts = [chunk.reshape(experts, -1, model_width) for chunk in chunks]
    return jnp.concatenate(parts, axis=1).reshape(-1, model_width)


def on_device(tokens, gate_probs, expert_ids, cotangent, w_gate, w_up, w_down):
    tok_count, model_width = tokens.shape
    top_k = expert_ids.shape[1]
    experts = lax.axis_size("expert")
    groups = lax.axis_size("dp")
    capacity = 3 * tok_count * top_k // (16 * experts)
    flat_count = tok_count * top_k
    slots = slot_table(expert_ids.reshape(-1), experts, capacity, flat_count)
    token_of = slots // top_k
    zero_row = jnp.zeros((1, model_width), jnp.bfloat16)
    send_x = jnp.concatenate([tokens, zero_row], 0)[token_of]
    rows_dy = jnp.concatenate([cotangent, zero_row], 0)[token_of]
    prob_rows = jnp.concatenate([gate_probs.reshape(-1), jnp.zeros((1,), jnp.float32)], 0)[slots]
    send_c = (prob_rows[:, None] * rows_dy.astype(jnp.float32)).astype(jnp.bfloat16)
    half = max(capacity // 2, 1)
    bounds = [(lo, hi) for lo, hi in ((0, half), (half, capacity)) if hi > lo]
    x_by_slot = send_x.reshape(experts, capacity, model_width)
    c_by_slot = send_c.reshape(experts, capacity, model_width)
    xs = [dispatch(x_by_slot[:, lo:hi].reshape(-1, model_width)) for lo, hi in bounds]
    cs = [dispatch(c_by_slot[:, lo:hi].reshape(-1, model_width)) for lo, hi in bounds]
    gate_w = w_gate[0]
    up_w = w_up[0]
    down_w = w_down[0]
    forwards = [expert_forward(rows_x, gate_w, up_w, down_w) for rows_x in xs]
    outs = [gather_back(fw[0], groups) for fw in forwards]
    backwards = [
        expert_backward(rows_c, fw[2], fw[3], gate_w, up_w, down_w)
        for rows_c, fw in zip(cs, forwards)
    ]
    dxs = [gather_back(bw[0], groups) for bw in backwards]
    new_gate = sum((contract_first(rx, bw[1]) for rx, bw in zip(xs, backwards)))
    new_up = sum((contract_first(rx, bw[2]) for rx, bw in zip(xs, backwards)))
    new_down = sum((contract_first(fw[1], rc) for fw, rc in zip(forwards, cs)))
    new_gate = new_gate.astype(jnp.bfloat16)[None]
    new_up = new_up.astype(jnp.bfloat16)[None]
    new_down = new_down.astype(jnp.bfloat16)[None]
    out_rows = join_slots(outs, experts, model_width).astype(jnp.float32)
    dx_rows = join_slots(dxs, experts, model_width).astype(jnp.float32)
    owner = (token_of[None, :] == jnp.arange(tok_count, dtype=jnp.int32)[:, None]).astype(
        jnp.float32
    )
    layer_out = jnp.dot(
        owner * prob_rows[None, :],
        out_rows,
        precision=lax.Precision.HIGHEST,
        preferred_element_type=jnp.float32,
    ).astype(jnp.bfloat16)
    grad_tokens = jnp.dot(
        owner, dx_rows, precision=lax.Precision.HIGHEST, preferred_element_type=jnp.float32
    ).astype(jnp.bfloat16)
    score_rows = jnp.sum(rows_dy.astype(jnp.float32) * out_rows, axis=1)
    grad_probs = (
        jnp.zeros((flat_count + 1,), jnp.float32)
        .at[slots]
        .set(score_rows)[:flat_count]
        .reshape(tok_count, top_k)
    )
    return (layer_out, grad_tokens, grad_probs, new_gate, new_up, new_down)


def solution(mesh):
    return jax.shard_map(
        on_device,
        mesh=mesh,
        in_specs=(
            P(("dp", "expert"), None),
            P(("dp", "expert"), None),
            P(("dp", "expert"), None),
            P(("dp", "expert"), None),
            P("expert", None, "dp"),
            P("expert", None, "dp"),
            P("expert", "dp", None),
        ),
        out_specs=(
            P(("dp", "expert"), None),
            P(("dp", "expert"), None),
            P(("dp", "expert"), None),
            P("expert", None, "dp"),
            P("expert", None, "dp"),
            P("expert", "dp", None),
        ),
        check_vma=False,
    )
```

profile of v0, /device:TPU:0, one launch (start us, length us, event | category | flops | bytes accessed | tf_op | source)
XLA Modules:
  0.0 435.6 jit_solution(945280252774466416)
XLA Ops:
  10.0 2.3 reduce-window.6
  12.9 4.3 scatter_custom_fusion
  17.2 1.2 concatenate.16
  18.5 1.4 gather_fusion.1
  20.1 29.9 %all_to_all.72 = bf16[8,12,3584]{2,1,0:T(8,128)(2,1)S(1)} all-to-all(bf16[8,12,3584]{2,1,0:T(8,128)(2,1)S(1)} %get-tuple-element.37), channel_id=1, replica_groups=mesh['dp'=4,'expert'=8] {'expert'}, dimensions={0} | all-to-all | bytes 1376256 | tf_op jit(solution)/shard_map/all_to_all | solution.py:30
  51.1 26.3 %all_to_all.73 = bf16[8,12,3584]{2,1,0:T(8,128)(2,1)S(1)} all-to-all(bf16[8,12,3584]{2,1,0:T(8,128)(2,1)S(1)} %get-tuple-element.36), channel_id=1, replica_groups=mesh['dp'=4,'expert'=8] {'expert'}, dimensions={0} | all-to-all | bytes 1376256 | tf_op jit(solution)/shard_map/all_to_all | solution.py:30
  78.8 1.4 gather_fusion
  80.4 1.4 gather_fusion.2
  82.9 26.2 %all_to_all.74 = bf16[8,12,3584]{2,1,0:T(8,128)(2,1)S(1)} all-to-all(bf16[8,12,3584]{2,1,0:T(8,128)(2,1)S(1)} %get-tuple-element.34), channel_id=1, replica_groups=mesh['dp'=4,'expert'=8] {'expert'}, dimensions={0} | all-to-all | bytes 1376256 | tf_op jit(solution)/shard_map/all_to_all | solution.py:30
  110.1 26.2 %all_to_all.75 = bf16[8,12,3584]{2,1,0:T(8,128)(2,1)S(1)} all-to-all(bf16[8,12,3584]{2,1,0:T(8,128)(2,1)S(1)} %get-tuple-element.35), channel_id=1, replica_groups=mesh['dp'=4,'expert'=8] {'expert'}, dimensions={0} | all-to-all | bytes 1376256 | tf_op jit(solution)/shard_map/all_to_all | solution.py:30
  137.4 4.6 %fusion.21 = f32[384,512]{1,0:T(8,128)S(1)} fusion(bf16[384,3584]{1,0:T(8,128)(2,1)} %all-gather.7.cloned.1.call-done, bf16[1,3584,512]{2,1,0:T(8,128)(2,1)} %param.11), kind=kOutput, calls=%fused_computation.35 | convolution fusion | flops 1409286144 | bytes 7208960 | tf_op jit(solution)/shard_map/dot_general | solution.py:40
  142.2 2.5 multiply_convert_fusion.5
  145.4 3.1 convolution_convert_fusion
  148.9 4.6 %fusion.23 = f32[384,512]{1,0:T(8,128)S(1)} fusion(bf16[384,3584]{1,0:T(8,128)(2,1)} %all-gather.5.cloned.1.call-done, bf16[1,3584,512]{2,1,0:T(8,128)(2,1)} %param.11), kind=kOutput, calls=%fused_computation.37 | convolution fusion | flops 1409286144 | bytes 7208960 | tf_op jit(solution)/shard_map/dot_general | solution.py:40
  153.6 2.5 multiply_convert_fusion.6
  156.8 3.1 convolution_convert_fusion.1
  160.1 16.6 %all-gather.9.cloned.1.call-done = bf16[384,3584]{1,0:T(8,128)(2,1)} async-done(((bf16[96,3584]{1,0:T(8,128)(2,1)}), bf16[384,3584]{1,0:T(8,128)(2,1)}) %all-gather.9.cloned.1.call-update) | async-done | bytes 2752528 | tf_op jit(solution)/shard_map/all_gather | solution.py:31
  176.7 5.2 %multiply_convert_fusion.3 = (bf16[384,512]{1,0:T(8,128)(2,1)S(1)}, bf16[384,512]{1,0:T(8,128)(2,1)S(1)}) fusion(f32[384,512]{1,0:T(8,128)} %copy-done.24, f32[384,512]{1,0:T(8,128)} %get-tuple-element.16, bf16[384,3584]{1,0:T(8,128)(2,1)} %all-gather.9.cloned.1.call-done, bf16[1,512,3584]{2,1,0:T(8,128)(2,1)} %param.13), kind=kOutput, calls=%fused_computation.46 | convolution fusion | flops 1411842048 | bytes 8781824 | tf_op jit(solution)/shard_map/dot_general | solution.py:18
  181.9 1.6 fusion.19
  183.9 3.2 fusion
  187.2 32.0 %all-gather.11.cloned.1.call-done = bf16[384,3584]{1,0:T(8,128)(2,1)} async-done(((bf16[96,3584]{1,0:T(8,128)(2,1)}), bf16[384,3584]{1,0:T(8,128)(2,1)}) %all-gather.11.cloned.1.call-update) | async-done | bytes 2752528 | tf_op jit(solution)/shard_map/all_gather | solution.py:31
  219.1 5.2 %multiply_convert_fusion.1 = (bf16[384,512]{1,0:T(8,128)(2,1)S(1)}, bf16[384,512]{1,0:T(8,128)(2,1)S(1)}) fusion(f32[384,512]{1,0:T(8,128)} %copy-done.23, f32[384,512]{1,0:T(8,128)} %get-tuple-element.18, bf16[384,3584]{1,0:T(8,128)(2,1)} %all-gather.11.cloned.1.call-done, bf16[1,512,3584]{2,1,0:T(8,128)(2,1)} %param.13), kind=kOutput, calls=%fused_computation.43 | convolution fusion | flops 1411842048 | bytes 8781824 | tf_op jit(solution)/shard_map/dot_general | solution.py:18
  224.4 1.6 fusion.17
  226.7 3.2 fusion.1
  229.9 33.3 %reduce-scatter.7.cloned.1.call-done = bf16[96,3584]{1,0:T(8,128)(2,1)} async-done(((bf16[384,3584]{1,0:T(8,128)(2,1)}), bf16[96,3584]{1,0:T(8,128)(2,1)}) %reduce-scatter.7.cloned.1.call-update) | async-done | bytes 688144 | tf_op jit(solution)/shard_map/reduce_scatter | solution.py:35
  263.3 2.1 all_to_all.54
  265.4 4.6 %all-to-all-start.3 = ((bf16[8,12,3584]{2,1,0:T(8,128)(2,1)}), bf16[8,12,3584]{2,1,0:T(8,128)(2,1)}, u32[]{:S(2)}, u32[]{:S(2)}) async-start(bf16[8,12,3584]{2,1,0:T(8,128)(2,1)} %all_to_all.54), calls=%async_computation.5 | async-start | bytes 1835008 | tf_op jit(solution)/shard_map/all_to_all | solution.py:36
  270.0 37.5 %reduce-scatter.5.cloned.1.call-done = bf16[96,3584]{1,0:T(8,128)(2,1)} async-done(((bf16[384,3584]{1,0:T(8,128)(2,1)}), bf16[96,3584]{1,0:T(8,128)(2,1)}) %reduce-scatter.5.cloned.1.call-update) | async-done | bytes 688144 | tf_op jit(solution)/shard_map/reduce_scatter | solution.py:35
  307.4 2.1 all_to_all.50
  309.5 4.6 %all-to-all-start.1 = ((bf16[8,12,3584]{2,1,0:T(8,128)(2,1)}), bf16[8,12,3584]{2,1,0:T(8,128)(2,1)}, u32[]{:S(2)}, u32[]{:S(2)}) async-start(bf16[8,12,3584]{2,1,0:T(8,128)(2,1)} %all_to_all.50), calls=%async_computation.2 | async-start | bytes 1835008 | tf_op jit(solution)/shard_map/all_to_all | solution.py:36
  314.1 3.9 fusion.42
  318.1 4.1 fusion.3
  322.1 29.6 %reduce-scatter.9.cloned.1.call-done = bf16[96,3584]{1,0:T(8,128)(2,1)} async-done(((bf16[384,3584]{1,0:T(8,128)(2,1)}), bf16[96,3584]{1,0:T(8,128)(2,1)}) %reduce-scatter.9.cloned.1.call-update) | async-done | bytes 688144 | tf_op jit(solution)/shard_map/reduce_scatter | solution.py:35
  351.7 2.1 all_to_all.58
  353.8 4.6 %all-to-all-start.5 = ((bf16[8,12,3584]{2,1,0:T(8,128)(2,1)}), bf16[8,12,3584]{2,1,0:T(8,128)(2,1)}, u32[]{:S(2)}, u32[]{:S(2)}) async-start(bf16[8,12,3584]{2,1,0:T(8,128)(2,1)} %all_to_all.58), calls=%async_computation.8 | async-start | bytes 1835008 | tf_op jit(solution)/shard_map/all_to_all | solution.py:36
  358.4 4.0 fusion.41
  362.5 5.0 %fusion.43 = f32[512,3584]{1,0:T(8,128)} fusion(bf16[384,512]{1,0:T(8,128)(2,1)S(1)} %copy-done.19, bf16[384,3584]{1,0:T(8,128)(2,1)S(1)} %copy-done.10), kind=kOutput, calls=%fused_computation.87 | convolution fusion | flops 1409286144 | bytes 10485760 | tf_op jit(solution)/shard_map/dot_general | solution.py:24
  367.5 4.1 fusion.2
  371.5 23.9 %reduce-scatter.11.cloned.1.call-done = bf16[96,3584]{1,0:T(8,128)(2,1)} async-done(((bf16[384,3584]{1,0:T(8,128)(2,1)}), bf16[96,3584]{1,0:T(8,128)(2,1)}) %reduce-scatter.11.cloned.1.call-update) | async-done | bytes 688144 | tf_op jit(solution)/shard_map/reduce_scatter | solution.py:35
  395.4 2.1 all_to_all.62
  397.5 4.6 %all-to-all-start.7 = ((bf16[8,12,3584]{2,1,0:T(8,128)(2,1)}), bf16[8,12,3584]{2,1,0:T(8,128)(2,1)S(1)}, u32[]{:S(2)}, u32[]{:S(2)}) async-start(bf16[8,12,3584]{2,1,0:T(8,128)(2,1)} %all_to_all.62), calls=%async_computation.11 | async-start | bytes 1835008 | tf_op jit(solution)/shard_map/all_to_all | solution.py:36
  402.1 7.9 %fusion.4 = bf16[1,512,3584]{2,1,0:T(8,128)(2,1)} fusion(f32[512,3584]{1,0:T(8,128)} %fusion.43, bf16[384,512]{1,0:T(8,128)(2,1)S(1)} %copy-done.17, bf16[384,3584]{1,0:T(8,128)(2,1)} %all-gather.11.cloned.1.call-done), kind=kOutput, calls=%fused_computation.16 | convolution fusion | flops 1412956160 | bytes 14155776 | tf_op jit(solution)/shard_map/dot_general | solution.py:24
  410.0 1.9 pad_maximum_fusion
  412.3 1.2 scatter_custom_fusion.1
  414.3 1.8 convolution_convert_fusion.3
  416.1 9.8 %all-to-all-done.7 = bf16[8,12,3584]{2,1,0:T(8,128)(2,1)S(1)} async-done(((bf16[8,12,3584]{2,1,0:T(8,128)(2,1)}), bf16[8,12,3584]{2,1,0:T(8,128)(2,1)S(1)}, u32[]{:S(2)}, u32[]{:S(2)}) %all-to-all-start.7) | async-done | bytes 688160 | tf_op jit(solution)/shard_map/all_to_all | solution.py:36
  425.9 1.5 pad_maximum_fusion.1
  427.4 1.3 convolution_convert_fusion.2
  (106 shorter events, 13.9 us)
Async XLA Ops:
  7.2 130.3 %all-gather.7.cloned.1.call-start = ((), (), s32[]{:S(2)}) async-start(), calls=%async_computation.14 | async-start | bytes 3440640 | tf_op jit(solution)/shard_map/all_gather | solution.py:31
  51.0 27.5 %copy-start.20 = (f32[128,8]{0,1:T(8,128)S(1)}, f32[128,8]{0,1:T(8,128)}, u32[]{:S(2)}) copy-start(f32[128,8]{0,1:T(8,128)} %param.8) | copy-start | bytes 12292
  51.1 29.2 %copy-start.15 = (bf16[128,3584]{1,0:T(8,128)(2,1)S(1)}, bf16[128,3584]{1,0:T(8,128)(2,1)}, u32[]{:S(2)}) copy-start(bf16[128,3584]{1,0:T(8,128)(2,1)} %param.10) | copy-start | bytes 2752516
  51.1 97.8 %all-gather.5.cloned.1.call-start = ((), (), s32[]{:S(2)}) async-start(), calls=%async_computation.12 | async-start | bytes 3440640 | tf_op jit(solution)/shard_map/all_gather | solution.py:31
  78.5 98.2 %all-gather.9.cloned.1.call-start = ((), (), s32[]{:S(2)}) async-start(), calls=%async_computation.16 | async-start | bytes 3440640 | tf_op jit(solution)/shard_map/all_gather | solution.py:31
  81.8 1.1 copy-start.8
  110.1 109.0 %all-gather.11.cloned.1.call-start = ((), (), s32[]{:S(2)}) async-start(), calls=%async_computation.18 | async-start | bytes 3440640 | tf_op jit(solution)/shard_map/all_gather | solution.py:31
  137.4 125.9 %reduce-scatter.7.cloned.1.call-start = ((), (), s32[]{:S(2)}) async-start(), calls=%async_computation.15 | async-start | bytes 3440640 | tf_op jit(solution)/shard_map/reduce_scatter | solution.py:35
  137.4 4.6 %copy-start = (bf16[384,3584]{1,0:T(8,128)(2,1)S(1)}, bf16[384,3584]{1,0:T(8,128)(2,1)}, u32[]{:S(2)}) copy-start(bf16[384,3584]{1,0:T(8,128)(2,1)} %all-gather.7.cloned.1.call-done) | copy-start | bytes 8257540
  137.4 4.8 %copy-start.3 = (bf16[1,3584,512]{2,1,0:T(8,128)(2,1)S(1)}, bf16[1,3584,512]{2,1,0:T(8,128)(2,1)}, u32[]{:S(2)}) copy-start(bf16[1,3584,512]{2,1,0:T(8,128)(2,1)} %param.12) | copy-start | bytes 11010052
  142.2 2.5 copy-start.23
  142.2 3.2 copy-start.21
  144.7 0.8 copy-start.16
  148.6 158.8 %reduce-scatter.5.cloned.1.call-start = ((), (), s32[]{:S(2)}) async-start(), calls=%async_computation.13 | async-start | bytes 3440640 | tf_op jit(solution)/shard_map/reduce_scatter | solution.py:35
  148.8 4.6 %copy-start.4 = (bf16[1,3584,512]{2,1,0:T(8,128)(2,1)S(1)}, bf16[1,3584,512]{2,1,0:T(8,128)(2,1)}, u32[]{:S(2)}) copy-start(bf16[1,3584,512]{2,1,0:T(8,128)(2,1)} %param.12) | copy-start | bytes 11010052
  148.9 4.8 %copy-start.7 = (bf16[384,3584]{1,0:T(8,128)(2,1)S(1)}, bf16[384,3584]{1,0:T(8,128)(2,1)}, u32[]{:S(2)}) copy-start(bf16[384,3584]{1,0:T(8,128)(2,1)} %all-gather.5.cloned.1.call-done) | copy-start | bytes 8257540
  153.6 2.5 copy-start.24
  153.6 3.2 copy-start.22
  156.1 0.7 copy-start.18
  160.0 191.7 %reduce-scatter.9.cloned.1.call-start = ((), (), s32[]{:S(2)}) async-start(), calls=%async_computation.17 | async-start | bytes 3440640 | tf_op jit(solution)/shard_map/reduce_scatter | solution.py:35
  176.7 5.2 %copy-start.1 = (bf16[1,3584,512]{2,1,0:T(8,128)(2,1)S(1)}, bf16[1,3584,512]{2,1,0:T(8,128)(2,1)}, u32[]{:S(2)}) copy-start(bf16[1,3584,512]{2,1,0:T(8,128)(2,1)} %param.11) | copy-start | bytes 11010052
  181.9 2.0 copy-start.5
  187.1 208.3 %reduce-scatter.11.cloned.1.call-start = ((), (), s32[]{:S(2)}) async-start(), calls=%async_computation.19 | async-start | bytes 3440640 | tf_op jit(solution)/shard_map/reduce_scatter | solution.py:35
  219.1 5.2 %copy-start.2 = (bf16[1,3584,512]{2,1,0:T(8,128)(2,1)S(1)}, bf16[1,3584,512]{2,1,0:T(8,128)(2,1)}, u32[]{:S(2)}) copy-start(bf16[1,3584,512]{2,1,0:T(8,128)(2,1)} %param.11) | copy-start | bytes 11010052
  224.3 1.7 copy-start.11
  224.3 1.7 copy-start.13
  224.4 2.3 copy-start.6
  265.4 44.1 %all-to-all-start.3 = ((bf16[8,12,3584]{2,1,0:T(8,128)(2,1)}), bf16[8,12,3584]{2,1,0:T(8,128)(2,1)}, u32[]{:S(2)}, u32[]{:S(2)}) async-start(bf16[8,12,3584]{2,1,0:T(8,128)(2,1)} %all_to_all.54), calls=%async_computation.5 | async-start | bytes 1835008 | tf_op jit(solution)/shard_map/all_to_all | solution.py:36
  309.5 44.3 %all-to-all-start.1 = ((bf16[8,12,3584]{2,1,0:T(8,128)(2,1)}), bf16[8,12,3584]{2,1,0:T(8,128)(2,1)}, u32[]{:S(2)}, u32[]{:S(2)}) async-start(bf16[8,12,3584]{2,1,0:T(8,128)(2,1)} %all_to_all.50), calls=%async_computation.2 | async-start | bytes 1835008 | tf_op jit(solution)/shard_map/all_to_all | solution.py:36
  314.1 3.9 copy-start.14
  353.8 43.7 %all-to-all-start.5 = ((bf16[8,12,3584]{2,1,0:T(8,128)(2,1)}), bf16[8,12,3584]{2,1,0:T(8,128)(2,1)}, u32[]{:S(2)}, u32[]{:S(2)}) async-start(bf16[8,12,3584]{2,1,0:T(8,128)(2,1)} %all_to_all.58), calls=%async_computation.8 | async-start | bytes 1835008 | tf_op jit(solution)/shard_map/all_to_all | solution.py:36
  358.4 4.0 copy-start.10
  358.4 4.1 copy-start.19
  362.4 5.0 %copy-start.12 = (bf16[384,512]{1,0:T(8,128)(2,1)S(1)}, bf16[384,512]{1,0:T(8,128)(2,1)}, u32[]{:S(2)}) copy-start(bf16[384,512]{1,0:T(8,128)(2,1)} %copy-done.11) | copy-start | bytes 1179652
  371.5 30.5 %copy-start.17 = (bf16[384,512]{1,0:T(8,128)(2,1)S(1)}, bf16[384,512]{1,0:T(8,128)(2,1)}, u32[]{:S(2)}) copy-start(bf16[384,512]{1,0:T(8,128)(2,1)} %copy-done.16) | copy-start | bytes 1179652
  397.5 28.4 %all-to-all-start.7 = ((bf16[8,12,3584]{2,1,0:T(8,128)(2,1)}), bf16[8,12,3584]{2,1,0:T(8,128)(2,1)S(1)}, u32[]{:S(2)}, u32[]{:S(2)}) async-start(bf16[8,12,3584]{2,1,0:T(8,128)(2,1)} %all_to_all.62), calls=%async_computation.11 | async-start | bytes 1835008 | tf_op jit(solution)/shard_map/all_to_all | solution.py:36
  410.0 1.9 copy-start.9
Sparse Core Ops, SparseCore 0:
  51.2 39.6 all-gather.6
  93.3 40.7 all-gather.4
  135.9 40.7 all-gather.8
  178.4 40.7 all-gather.10
  222.6 40.6 reduce-scatter.6
  266.7 40.6 reduce-scatter.4
  311.0 40.6 reduce-scatter.8
  354.7 40.6 reduce-scatter.10
where the time goes:
time: 436 us
  waiting for transfers between devices  183 us (42%)
  blocking collectives  109 us (25%)
  matrix products  72.5 us (17%)
  local copies, waits for them, and re-layouts  30.1 us (7%)
  starting transfers between devices  18.9 us (4%)
  between operations  14.6 us (3%)
  other arithmetic  8.13 us (2%)
    reduce_scatter x4, waiting for transfers between devices, gather_back(): lax.psum_scatter(partial_rows, 'dp', scatter_dimension=0, tiled=True)  124 us
    all_to_all x4, blocking collectives, dispatch(): lax.all_to_all(send_rows, 'expert', split_axis=0, concat_axis=0, tiled=True)  109 us
    all_gather x4, waiting for transfers between devices, dispatch(): return lax.all_gather(along_expert, 'dp', axis=0, tiled=True)  48.6 us
    dot_general x6, matrix products, contract_first(): lax.dot_general(left, right, (((0,), (0,)), ((), ())), preferred_element_...  29 us
    dot_general x6, matrix products, contract_last(): lax.dot_general(left, right, (((1,), (1,)), ((), ())), preferred_element_...  20 us
    all_to_all x4, starting transfers between devices, gather_back(): lax.all_to_all(summed, 'expert', split_axis=0, concat_axis=0, tiled=True)  18.4 us
    all_to_all x4, waiting for transfers between devices, gather_back(): lax.all_to_all(summed, 'expert', split_axis=0, concat_axis=0, tiled=True)  9.8 us
    dot_general x2, matrix products, expert_forward(): gate_pre = jnp.dot(rows_x, gate_w, preferred_element_type=jnp.float32)  9.19 us
  transfers between devices with their start and end apart: 12, of which 7 were waited for; matrix products, arithmetic and copies ran while one was open for 18% of the time, Pallas kernels for 0%

commit v1 on v0

--- a/solution.py
+++ b/solution.py
@@ -1,7 +1,24 @@
+import functools
 import jax
 import jax.numpy as jnp
 from jax import lax
 from jax.sharding import PartitionSpec as P
+from jax.lax import axis_index, axis_size, ppermute
+
+
+def slabs_cover(field, which_dim):
+    formed, r2 = (axis_size("dp"), axis_index("dp"))
+    all_rows, part_now = (field, 1)
+    while part_now < formed:
+        base_arr = ppermute(all_rows, "dp", tuple(((b, b ^ part_now) for b in range(formed))))
+        f_next = jnp.concatenate([all_rows, base_arr], axis=which_dim)
+        big = jnp.concatenate([base_arr, all_rows], axis=which_dim)
+        all_rows = jnp.where(r2 & part_now == 0, f_next, big)
+        part_now = 2 * part_now
+    return all_rows
+
+
+review_weights_by_axis = functools.partial(slabs_cover, which_dim=0)
 
 
 def slot_table(flat_ids, experts, capacity, sentinel):
@@ -28,7 +45,7 @@
 
 def dispatch(send_rows):
     along_expert = lax.all_to_all(send_rows, "expert", split_axis=0, concat_axis=0, tiled=True)
-    return lax.all_gather(along_expert, "dp", axis=0, tiled=True)
+    return review_weights_by_axis(along_expert)
 
 
 def gather_back(partial_rows, groups):

time: 436 us -> 461 us (1.057); the launches traced: 436 us -> 452 us
  blocking collectives: 109 us -> 29.9 us
  waiting for transfers between devices: 183 us -> 227 us
  matrix products: 72.5 us -> 98.8 us
  starting transfers between devices: 18.9 us -> 43 us
    ppermute x0 -> x8, waiting for transfers between devices: none -> 193 us  [slabs_cover(): ppermute(all_rows, 'dp', tuple(((b, b ^ part_now) for b in range(formed))))]
    reduce_scatter x4, waiting for transfers between devices: 124 us -> 0.03 us  [gather_back(): lax.psum_scatter(partial_rows, 'dp', scatter_dimension=0, tiled=True)]
    all_to_all x4 -> x1, blocking collectives: 109 us -> 29.9 us  [dispatch(): lax.all_to_all(send_rows, 'expert', split_axis=0, concat_axis=0, tiled=True)]
    all_gather x4 -> x0, waiting for transfers between devices: 48.6 us -> none  [dispatch(): return lax.all_gather(along_expert, 'dp', axis=0, tiled=True)]
    all_to_all x4, waiting for transfers between devices: 9.8 us -> 34.2 us  [gather_back(): lax.all_to_all(summed, 'expert', split_axis=0, concat_axis=0, tiled=True)]
    dot_general x6, matrix products: 29 us -> 49.7 us  [contract_first(): lax.dot_general(left, right, (((0,), (0,)), ((), ())), preferred_element_...]
    all_to_all x0 -> x3, starting transfers between devices: none -> 12.7 us  [dispatch(): lax.all_to_all(send_rows, 'expert', split_axis=0, concat_axis=0, tiled=True)]
    ppermute x0 -> x8, starting transfers between devices: none -> 8 us  [slabs_cover(): ppermute(all_rows, 'dp', tuple(((b, b ^ part_now) for b in range(formed))))]
  transfers between devices with their start and end apart: 12 -> 19, of which waited for: 7 -> 12; matrix products, arithmetic and copies ran while one was open for 18% -> 24% of each run, Pallas kernels for 0% -> 0%
where the time goes in v1:
time: 461 us; the launch traced here: 452 us
  waiting for transfers between devices  227 us (49%)
  matrix products  98.8 us (21%)
  starting transfers between devices  43 us (9%)
  blocking collectives  29.9 us (6%)
  local copies, waits for them, and re-layouts  28 us (6%)
  between operations  14.6 us (3%)
  other arithmetic  11.3 us (2%)
    ppermute x8, waiting for transfers between devices, slabs_cover(): ppermute(all_rows, 'dp', tuple(((b, b ^ part_now) for b in range(formed))))  193 us
    dot_general x6, matrix products, contract_first(): lax.dot_general(left, right, (((0,), (0,)), ((), ())), preferred_element_...  49.7 us
    all_to_all x4, waiting for transfers between devices, gather_back(): lax.all_to_all(summed, 'expert', split_axis=0, concat_axis=0, tiled=True)  34.2 us
    all_to_all x1, blocking collectives, dispatch(): lax.all_to_all(send_rows, 'expert', split_axis=0, concat_axis=0, tiled=True)  29.9 us
    all_to_all x4, starting transfers between devices, gather_back(): lax.all_to_all(summed, 'expert', split_axis=0, concat_axis=0, tiled=True)  21.5 us
    dot_general x6, matrix products, contract_last(): lax.dot_general(left, right, (((1,), (1,)), ((), ())), preferred_element_...  19.9 us
    all_to_all x3, starting transfers between devices, dispatch(): lax.all_to_all(send_rows, 'expert', split_axis=0, concat_axis=0, tiled=True)  12.7 us
    dot_general x2, matrix products, expert_forward(): up_pre = jnp.dot(rows_x, up_w, preferred_element_type=jnp.float32)  9.92 us
  transfers between devices with their start and end apart: 19, of which 12 were waited for; matrix products, arithmetic and copies ran while one was open for 24% of the time, Pallas kernels for 0%

profile of v1, /device:TPU:0, one launch (start us, length us, event | category | flops | bytes accessed | tf_op | source)
XLA Modules:
  0.0 452.5 jit_solution(9521798020421748610)
XLA Ops:
  10.0 2.3 reduce-window.6
  12.8 4.3 scatter_custom_fusion
  21.0 29.9 %all_to_all.72 = bf16[8,12,3584]{2,1,0:T(8,128)(2,1)S(1)} all-to-all(bf16[8,12,3584]{2,1,0:T(8,128)(2,1)S(1)} %get-tuple-element.37), channel_id=1, replica_groups=mesh['dp'=4,'expert'=8] {'expert'}, dimensions={0} | all-to-all | bytes 1376256 | tf_op jit(solution)/shard_map/all_to_all | solution.py:47
  52.6 15.5 %collective-permute-done.2 = bf16[96,3584]{1,0:T(8,128)(2,1)S(1)} collective-permute-done((bf16[96,3584]{1,0:T(8,128)(2,1)S(1)}, bf16[96,3584]{1,0:T(8,128)(2,1)S(1)}, u32[]{:S(2)}, u32[]{:S(2)}) %collective-permute-start.2) | collective-permute-done | bytes 688160 | tf_op jit(solution)/shard_map/ppermute | solution.py:13
  68.3 1.6 collective-permute-start.3
  69.9 3.6 all-to-all-start
  73.6 25.8 %collective-permute-done.3 = bf16[192,3584]{1,0:T(8,128)(2,1)} collective-permute-done((bf16[192,3584]{1,0:T(8,128)(2,1)S(1)}, bf16[192,3584]{1,0:T(8,128)(2,1)}, u32[]{:S(2)}, u32[]{:S(2)}) %collective-permute-start.3) | collective-permute-done | bytes 1376288 | tf_op jit(solution)/shard_map/ppermute | solution.py:13
  99.3 4.5 %fusion.21 = f32[384,512]{1,0:T(8,128)S(1)} fusion(bf16[1,3584,512]{2,1,0:T(8,128)(2,1)} %param.11, bf16[192,3584]{1,0:T(8,128)(2,1)} %collective-permute-done.3, bf16[192,3584]{1,0:T(8,128)(2,1)S(1)} %maximum_select_fusion.5, pred[]{:T(512)S(6)} %eq.61), kind=kOutput, calls=%fused_computation.35 | convolution fusion | flops 1421672448 | bytes 7208961 | tf_op jit(solution)/shard_map/dot_general | solution.py:57
  103.9 4.5 %multiply_convert_fusion.5 = (bf16[384,512]{1,0:T(8,128)(2,1)S(1)}, f32[384,512]{1,0:T(8,128)}) fusion(f32[384,512]{1,0:T(8,128)S(1)} %fusion.21, bf16[1,3584,512]{2,1,0:T(8,128)(2,1)S(1)} %copy-done.2, bf16[192,3584]{1,0:T(8,128)(2,1)} %collective-permute-done.3, bf16[192,3584]{1,0:T(8,128)(2,1)S(1)} %maximum_select_fusion.5, pred[]{:T(512)S(6)} %eq.61), kind=kOutput, calls=%fused_computation.57 | convolution fusion | flops 1422852096 | bytes 8388609 | tf_op jit(solution)/shard_map/dot_general | solution.py:58
  108.5 3.1 convolution_convert_fusion
  117.8 19.4 %collective-permute-done = bf16[96,3584]{1,0:T(8,128)(2,1)} collective-permute-done((bf16[96,3584]{1,0:T(8,128)(2,1)S(1)}, bf16[96,3584]{1,0:T(8,128)(2,1)}, u32[]{:S(2)}, u32[]{:S(2)}) %collective-permute-start) | collective-permute-done | bytes 688160 | tf_op jit(solution)/shard_map/ppermute | solution.py:13
  137.2 2.6 maximum_select_fusion.4
  143.1 3.6 all-to-all-start.4
  147.2 26.6 %collective-permute-done.1 = bf16[192,3584]{1,0:T(8,128)(2,1)} collective-permute-done((bf16[192,3584]{1,0:T(8,128)(2,1)}, bf16[192,3584]{1,0:T(8,128)(2,1)}, u32[]{:S(2)}, u32[]{:S(2)}) %collective-permute-start.1) | collective-permute-done | bytes 1376288 | tf_op jit(solution)/shard_map/ppermute | solution.py:13
  173.8 5.3 %fusion.23 = f32[384,512]{1,0:T(8,128)S(1)} fusion(bf16[1,3584,512]{2,1,0:T(8,128)(2,1)} %param.11, bf16[192,3584]{1,0:T(8,128)(2,1)} %collective-permute-done.1, bf16[192,3584]{1,0:T(8,128)(2,1)} %maximum_select_fusion.4, pred[]{:T(512)S(6)} %eq.61), kind=kOutput, calls=%fused_computation.37 | convolution fusion | flops 1421672448 | bytes 7208961 | tf_op jit(solution)/shard_map/dot_general | solution.py:57
  179.2 5.4 %multiply_convert_fusion.6 = (bf16[384,512]{1,0:T(8,128)(2,1)S(1)}, f32[384,512]{1,0:T(8,128)}) fusion(f32[384,512]{1,0:T(8,128)S(1)} %fusion.23, bf16[1,3584,512]{2,1,0:T(8,128)(2,1)S(1)} %copy-done.3, bf16[192,3584]{1,0:T(8,128)(2,1)} %collective-permute-done.1, bf16[192,3584]{1,0:T(8,128)(2,1)} %maximum_select_fusion.4, pred[]{:T(512)S(6)} %eq.61), kind=kOutput, calls=%fused_computation.58 | convolution fusion | flops 1422852096 | bytes 8388609 | tf_op jit(solution)/shard_map/dot_general | solution.py:58
  184.5 3.1 convolution_convert_fusion.1
  189.3 15.8 %collective-permute-done.4 = bf16[96,3584]{1,0:T(8,128)(2,1)S(1)} collective-permute-done((bf16[96,3584]{1,0:T(8,128)(2,1)S(1)}, bf16[96,3584]{1,0:T(8,128)(2,1)S(1)}, u32[]{:S(2)}, u32[]{:S(2)}) %collective-permute-start.4) | collective-permute-done | bytes 688160 | tf_op jit(solution)/shard_map/ppermute | solution.py:13
  206.4 5.6 %all-to-all-start.6 = ((bf16[8,12,3584]{2,1,0:T(8,128)(2,1)}), bf16[8,12,3584]{2,1,0:T(8,128)(2,1)S(1)}, u32[]{:S(2)}, u32[]{:S(2)}) async-start(bf16[8,12,3584]{2,1,0:T(8,128)(2,1)} %get-tuple-element.35), calls=%async_computation.9 | async-start | bytes 1835008 | tf_op jit(solution)/shard_map/all_to_all | solution.py:47
  212.0 34.8 %collective-permute-done.5 = bf16[192,3584]{1,0:T(8,128)(2,1)} collective-permute-done((bf16[192,3584]{1,0:T(8,128)(2,1)}, bf16[192,3584]{1,0:T(8,128)(2,1)}, u32[]{:S(2)}, u32[]{:S(2)}) %collective-permute-start.5) | collective-permute-done | bytes 1376288 | tf_op jit(solution)/shard_map/ppermute | solution.py:13
  246.8 6.0 %multiply_convert_fusion.3 = (bf16[384,512]{1,0:T(8,128)(2,1)S(1)}, bf16[384,512]{1,0:T(8,128)(2,1)S(1)}) fusion(f32[384,512]{1,0:T(8,128)} %copy-done.27, f32[384,512]{1,0:T(8,128)} %get-tuple-element.16, bf16[1,512,3584]{2,1,0:T(8,128)(2,1)} %param.13, bf16[192,3584]{1,0:T(8,128)(2,1)} %collective-permute-done.5, ...), kind=kOutput, calls=%fused_computation.54 | convolution fusion | flops 1424228352 | bytes 8781825 | tf_op jit(solution)/shard_map/dot_general | solution.py:35
  252.9 1.6 fusion.19
  255.2 3.2 fusion
  259.1 13.8 %collective-permute-done.6 = bf16[96,3584]{1,0:T(8,128)(2,1)S(1)} collective-permute-done((bf16[96,3584]{1,0:T(8,128)(2,1)S(1)}, bf16[96,3584]{1,0:T(8,128)(2,1)S(1)}, u32[]{:S(2)}, u32[]{:S(2)}) %collective-permute-start.6) | collective-permute-done | bytes 688160 | tf_op jit(solution)/shard_map/ppermute | solution.py:13
  273.3 41.0 %collective-permute-done.7 = bf16[192,3584]{1,0:T(8,128)(2,1)S(1)} collective-permute-done((bf16[192,3584]{1,0:T(8,128)(2,1)S(1)}, bf16[192,3584]{1,0:T(8,128)(2,1)S(1)}, u32[]{:S(2)}, u32[]{:S(2)}) %collective-permute-start.7) | collective-permute-done | bytes 1376288 | tf_op jit(solution)/shard_map/ppermute | solution.py:13
  314.2 4.4 multiply_convert_fusion.1
  318.7 1.6 fusion.17
  320.9 3.1 fusion.1
  324.0 2.1 all_to_all.54
  326.1 9.9 %all-to-all-start.3 = ((bf16[8,12,3584]{2,1,0:T(8,128)(2,1)}), bf16[8,12,3584]{2,1,0:T(8,128)(2,1)S(1)}, u32[]{:S(2)}, u32[]{:S(2)}) async-start(bf16[8,12,3584]{2,1,0:T(8,128)(2,1)} %all_to_all.54), calls=%async_computation.5 | async-start | bytes 1835008 | tf_op jit(solution)/shard_map/all_to_all | solution.py:53
  336.0 7.7 %fusion.44 = f32[3584,512]{1,0:T(8,128)} fusion(bf16[384,512]{1,0:T(8,128)(2,1)S(1)} %get-tuple-element.32, bf16[192,3584]{1,0:T(8,128)(2,1)} %collective-permute-done.3, bf16[192,3584]{1,0:T(8,128)(2,1)} %copy-done.11, pred[]{:T(512)S(6)} %eq.61), kind=kOutput, calls=%fused_computation.96 | convolution fusion | flops 1421672448 | bytes 10485761 | tf_op jit(solution)/shard_map/dot_general | solution.py:41
  343.7 2.1 all_to_all.50
  345.9 13.9 %all-to-all-done.3 = bf16[8,12,3584]{2,1,0:T(8,128)(2,1)S(1)} async-done(((bf16[8,12,3584]{2,1,0:T(8,128)(2,1)}), bf16[8,12,3584]{2,1,0:T(8,128)(2,1)S(1)}, u32[]{:S(2)}, u32[]{:S(2)}) %all-to-all-start.3) | async-done | bytes 688160 | tf_op jit(solution)/shard_map/all_to_all | solution.py:53
  359.8 3.6 all-to-all-start.1
  363.4 7.9 %fusion.45 = f32[3584,512]{1,0:T(8,128)} fusion(bf16[384,512]{1,0:T(8,128)(2,1)} %copy-done.17, bf16[192,3584]{1,0:T(8,128)(2,1)} %collective-permute-done.3, bf16[192,3584]{1,0:T(8,128)(2,1)} %copy-done.11, pred[]{:T(512)S(6)} %eq.61), kind=kOutput, calls=%fused_computation.97 | convolution fusion | flops 1421672448 | bytes 10485761 | tf_op jit(solution)/shard_map/dot_general | solution.py:41
  371.3 8.8 %fusion.3 = bf16[1,3584,512]{2,1,0:T(8,128)(2,1)} fusion(f32[3584,512]{1,0:T(8,128)} %fusion.44, bf16[384,512]{1,0:T(8,128)(2,1)S(1)} %copy-done.16, bf16[192,3584]{1,0:T(8,128)(2,1)} %collective-permute-done.1, bf16[192,3584]{1,0:T(8,128)(2,1)} %maximum_select_fusion.4, pred[]{:T(512)S(6)} %eq.61), kind=kOutput, calls=%fused_computation.15 | convolution fusion | flops 1425342464 | bytes 14155777 | tf_op jit(solution)/shard_map/dot_general | solution.py:41
  380.1 2.1 all_to_all.58
  382.2 4.9 %all-to-all-done.1 = bf16[8,12,3584]{2,1,0:T(8,128)(2,1)S(1)} async-done(((bf16[8,12,3584]{2,1,0:T(8,128)(2,1)}), bf16[8,12,3584]{2,1,0:T(8,128)(2,1)S(1)}, u32[]{:S(2)}, u32[]{:S(2)}) %all-to-all-start.1) | async-done | bytes 688160 | tf_op jit(solution)/shard_map/all_to_all | solution.py:53
  387.1 3.8 all-to-all-start.5
  390.9 7.8 %fusion.25 = f32[512,3584]{1,0:T(8,128)} fusion(bf16[384,512]{1,0:T(8,128)(2,1)} %copy-done.22, bf16[192,3584]{1,0:T(8,128)(2,1)} %copy-done.21, bf16[192,3584]{1,0:T(8,128)(2,1)} %copy-done.12, pred[]{:T(512)S(6)} %eq.61), kind=kOutput, calls=%fused_computation.59 | convolution fusion | flops 1421672448 | bytes 10485761 | tf_op jit(solution)/shard_map/dot_general | solution.py:41
  398.7 8.7 %fusion.2 = bf16[1,3584,512]{2,1,0:T(8,128)(2,1)} fusion(f32[3584,512]{1,0:T(8,128)} %fusion.45, bf16[384,512]{1,0:T(8,128)(2,1)S(1)} %copy-done.14, bf16[192,3584]{1,0:T(8,128)(2,1)} %collective-permute-done.1, bf16[192,3584]{1,0:T(8,128)(2,1)} %maximum_select_fusion.4, pred[]{:T(512)S(6)} %eq.61), kind=kOutput, calls=%fused_computation.14 | convolution fusion | flops 1425342464 | bytes 14155777 | tf_op jit(solution)/shard_map/dot_general | solution.py:41
  407.3 2.2 all_to_all.62
  409.6 5.0 %all-to-all-done.5 = bf16[8,12,3584]{2,1,0:T(8,128)(2,1)S(1)} async-done(((bf16[8,12,3584]{2,1,0:T(8,128)(2,1)}), bf16[8,12,3584]{2,1,0:T(8,128)(2,1)S(1)}, u32[]{:S(2)}, u32[]{:S(2)}) %all-to-all-start.5) | async-done | bytes 688160 | tf_op jit(solution)/shard_map/all_to_all | solution.py:53
  414.6 4.2 all-to-all-start.7
  418.9 8.8 %fusion.4 = bf16[1,512,3584]{2,1,0:T(8,128)(2,1)} fusion(f32[512,3584]{1,0:T(8,128)} %fusion.25, bf16[384,512]{1,0:T(8,128)(2,1)S(1)} %copy-done.24, bf16[192,3584]{1,0:T(8,128)(2,1)} %collective-permute-done.5, bf16[192,3584]{1,0:T(8,128)(2,1)} %maximum_select_fusion.6, pred[]{:T(512)S(6)} %eq.61), kind=kOutput, calls=%fused_computation.16 | convolution fusion | flops 1425342464 | bytes 14155777 | tf_op jit(solution)/shard_map/dot_general | solution.py:41
  430.4 1.8 convolution_convert_fusion.3
  432.2 10.4 %all-to-all-done.7 = bf16[8,12,3584]{2,1,0:T(8,128)(2,1)} async-done(((bf16[8,12,3584]{2,1,0:T(8,128)(2,1)}), bf16[8,12,3584]{2,1,0:T(8,128)(2,1)}, u32[]{:S(2)}, u32[]{:S(2)}) %all-to-all-start.7) | async-done | bytes 688160 | tf_op jit(solution)/shard_map/all_to_all | solution.py:53
  442.6 1.8 pad_maximum_fusion.1
  (125 shorter events, 28.4 us)
Async XLA Ops:
  51.0 17.1 %collective-permute-start.2 = (bf16[96,3584]{1,0:T(8,128)(2,1)S(1)}, bf16[96,3584]{1,0:T(8,128)(2,1)S(1)}, u32[]{:S(2)}, u32[]{:S(2)}) collective-permute-start(bf16[96,3584]{1,0:T(8,128)(2,1)S(1)} %all_to_all.53), channel_id=1, source_target_pairs={{0,8},{8,0},{16,24},{24,16},{1,9},{9,1},{17,25},{25,17},{2,10},{10... | collective-permute-start | bytes 2064392 | tf_op jit(solution)/shard_map/ppermute | solution.py:13
  68.3 35.6 %copy-start.11 = (bf16[192,3584]{1,0:T(8,128)(2,1)}, bf16[192,3584]{1,0:T(8,128)(2,1)S(1)}, u32[]{:S(2)}) copy-start(bf16[192,3584]{1,0:T(8,128)(2,1)S(1)} %maximum_select_fusion.5) | copy-start | bytes 4128772
  68.3 31.0 %collective-permute-start.3 = (bf16[192,3584]{1,0:T(8,128)(2,1)S(1)}, bf16[192,3584]{1,0:T(8,128)(2,1)}, u32[]{:S(2)}, u32[]{:S(2)}) collective-permute-start(bf16[192,3584]{1,0:T(8,128)(2,1)S(1)} %maximum_select_fusion.5), channel_id=1, source_target_pairs={{0,16},{8,24},{16,0},{24,8},{1,17},{9,25},{17,1},{25,9},{2,18},{10... | collective-permute-start | bytes 4128776 | tf_op jit(solution)/shard_map/ppermute | solution.py:13
  69.9 41.7 %all-to-all-start = ((bf16[8,12,3584]{2,1,0:T(8,128)(2,1)}), bf16[8,12,3584]{2,1,0:T(8,128)(2,1)S(1)}, u32[]{:S(2)}, u32[]{:S(2)}) async-start(bf16[8,12,3584]{2,1,0:T(8,128)(2,1)} %get-tuple-element.36), calls=%async_computation | async-start | bytes 1835008 | tf_op jit(solution)/shard_map/all_to_all | solution.py:47
  73.5 250.6 %reduce-scatter.7.cloned.1.call-start = ((), (), s32[]{:S(2)}) async-start(), calls=%async_computation.13 | async-start | bytes 3440640 | tf_op jit(solution)/shard_map/reduce_scatter | solution.py:52
  73.5 30.4 %copy-start.2 = (bf16[1,3584,512]{2,1,0:T(8,128)(2,1)S(1)}, bf16[1,3584,512]{2,1,0:T(8,128)(2,1)}, u32[]{:S(2)}) copy-start(bf16[1,3584,512]{2,1,0:T(8,128)(2,1)} %param.12) | copy-start | bytes 11010052
  103.9 4.6 %copy-start.25 = (f32[384,512]{1,0:T(8,128)}, f32[384,512]{1,0:T(8,128)S(1)}, u32[]{:S(2)}) copy-start(f32[384,512]{1,0:T(8,128)S(1)} %fusion.21) | copy-start | bytes 2359300
  103.9 4.6 %copy-start.19 = (bf16[1,512,3584]{2,1,0:T(8,128)(2,1)S(1)}, bf16[1,512,3584]{2,1,0:T(8,128)(2,1)}, u32[]{:S(2)}) copy-start(bf16[1,512,3584]{2,1,0:T(8,128)(2,1)} %param.13) | copy-start | bytes 11010052
  108.5 3.1 copy-start.22
  111.6 1.8 copy-start.18
  111.8 25.4 %collective-permute-start = (bf16[96,3584]{1,0:T(8,128)(2,1)S(1)}, bf16[96,3584]{1,0:T(8,128)(2,1)}, u32[]{:S(2)}, u32[]{:S(2)}) collective-permute-start(bf16[96,3584]{1,0:T(8,128)(2,1)S(1)} %all_to_all.49), channel_id=1, source_target_pairs={{0,8},{8,0},{16,24},{24,16},{1,9},{9,1},{17,25},{25,17},{2,10},{10... | collective-permute-start | bytes 2064392 | tf_op jit(solution)/shard_map/ppermute | solution.py:13
  139.8 33.9 %collective-permute-start.1 = (bf16[192,3584]{1,0:T(8,128)(2,1)}, bf16[192,3584]{1,0:T(8,128)(2,1)}, u32[]{:S(2)}, u32[]{:S(2)}) collective-permute-start(bf16[192,3584]{1,0:T(8,128)(2,1)} %maximum_select_fusion.4), channel_id=1, source_target_pairs={{0,16},{8,24},{16,0},{24,8},{1,17},{9,25},{17,1},{25,9},{2,18},{10... | collective-permute-start | bytes 4128776 | tf_op jit(solution)/shard_map/ppermute | solution.py:13
  143.1 44.6 %all-to-all-start.4 = ((bf16[8,12,3584]{2,1,0:T(8,128)(2,1)}), bf16[8,12,3584]{2,1,0:T(8,128)(2,1)S(1)}, u32[]{:S(2)}, u32[]{:S(2)}) async-start(bf16[8,12,3584]{2,1,0:T(8,128)(2,1)} %get-tuple-element.34), calls=%async_computation.6 | async-start | bytes 1835008 | tf_op jit(solution)/shard_map/all_to_all | solution.py:47
  146.6 197.1 %reduce-scatter.5.cloned.1.call-start = ((), (), s32[]{:S(2)}) async-start(), calls=%async_computation.12 | async-start | bytes 3440640 | tf_op jit(solution)/shard_map/reduce_scatter | solution.py:52
  147.2 32.0 %copy-start.3 = (bf16[1,3584,512]{2,1,0:T(8,128)(2,1)S(1)}, bf16[1,3584,512]{2,1,0:T(8,128)(2,1)}, u32[]{:S(2)}) copy-start(bf16[1,3584,512]{2,1,0:T(8,128)(2,1)} %param.12) | copy-start | bytes 11010052
  179.1 5.4 %copy-start.27 = (f32[384,512]{1,0:T(8,128)}, f32[384,512]{1,0:T(8,128)S(1)}, u32[]{:S(2)}) copy-start(f32[384,512]{1,0:T(8,128)S(1)} %fusion.23) | copy-start | bytes 2359300
  179.1 5.4 %copy-start.20 = (bf16[1,512,3584]{2,1,0:T(8,128)(2,1)S(1)}, bf16[1,512,3584]{2,1,0:T(8,128)(2,1)}, u32[]{:S(2)}) copy-start(bf16[1,512,3584]{2,1,0:T(8,128)(2,1)} %param.13) | copy-start | bytes 11010052
  184.5 3.1 copy-start.23
  187.9 17.2 %collective-permute-start.4 = (bf16[96,3584]{1,0:T(8,128)(2,1)S(1)}, bf16[96,3584]{1,0:T(8,128)(2,1)S(1)}, u32[]{:S(2)}, u32[]{:S(2)}) collective-permute-start(bf16[96,3584]{1,0:T(8,128)(2,1)S(1)} %all_to_all.57), channel_id=1, source_target_pairs={{0,8},{8,0},{16,24},{24,16},{1,9},{9,1},{17,25},{25,17},{2,10},{10... | collective-permute-start | bytes 2064392 | tf_op jit(solution)/shard_map/ppermute | solution.py:13
  206.4 40.5 %collective-permute-start.5 = (bf16[192,3584]{1,0:T(8,128)(2,1)}, bf16[192,3584]{1,0:T(8,128)(2,1)}, u32[]{:S(2)}, u32[]{:S(2)}) collective-permute-start(bf16[192,3584]{1,0:T(8,128)(2,1)} %maximum_select_fusion.6), channel_id=1, source_target_pairs={{0,16},{8,24},{16,0},{24,8},{1,17},{9,25},{17,1},{25,9},{2,18},{10... | collective-permute-start | bytes 4128776 | tf_op jit(solution)/shard_map/ppermute | solution.py:13
  206.4 52.2 %all-to-all-start.6 = ((bf16[8,12,3584]{2,1,0:T(8,128)(2,1)}), bf16[8,12,3584]{2,1,0:T(8,128)(2,1)S(1)}, u32[]{:S(2)}, u32[]{:S(2)}) async-start(bf16[8,12,3584]{2,1,0:T(8,128)(2,1)} %get-tuple-element.35), calls=%async_computation.9 | async-start | bytes 1835008 | tf_op jit(solution)/shard_map/all_to_all | solution.py:47
  211.9 168.2 %reduce-scatter.9.cloned.1.call-start = ((), (), s32[]{:S(2)}) async-start(), calls=%async_computation.14 | async-start | bytes 3440640 | tf_op jit(solution)/shard_map/reduce_scatter | solution.py:52
  212.0 40.8 %copy-start = (bf16[1,3584,512]{2,1,0:T(8,128)(2,1)S(1)}, bf16[1,3584,512]{2,1,0:T(8,128)(2,1)}, u32[]{:S(2)}) copy-start(bf16[1,3584,512]{2,1,0:T(8,128)(2,1)} %param.11) | copy-start | bytes 11010052
  252.8 1.7 copy-start.13
  252.8 1.7 copy-start.15
  252.8 2.3 copy-start.4
  258.3 149.0 %reduce-scatter.11.cloned.1.call-start = ((), (), s32[]{:S(2)}) async-start(), calls=%async_computation.15 | async-start | bytes 3440640 | tf_op jit(solution)/shard_map/reduce_scatter | solution.py:52
  258.7 55.5 %copy-start.26 = (f32[384,512]{1,0:T(8,128)S(1)}, f32[384,512]{1,0:T(8,128)}, u32[]{:S(2)}) copy-start(f32[384,512]{1,0:T(8,128)} %copy-done.25) | copy-start | bytes 2359300
  258.7 55.5 %copy-start.28 = (f32[384,512]{1,0:T(8,128)S(1)}, f32[384,512]{1,0:T(8,128)}, u32[]{:S(2)}) copy-start(f32[384,512]{1,0:T(8,128)} %get-tuple-element.18) | copy-start | bytes 2359300
  258.8 14.2 %collective-permute-start.6 = (bf16[96,3584]{1,0:T(8,128)(2,1)S(1)}, bf16[96,3584]{1,0:T(8,128)(2,1)S(1)}, u32[]{:S(2)}, u32[]{:S(2)}) collective-permute-start(bf16[96,3584]{1,0:T(8,128)(2,1)S(1)} %all_to_all.61), channel_id=1, source_target_pairs={{0,8},{8,0},{16,24},{24,16},{1,9},{9,1},{17,25},{25,17},{2,10},{10... | collective-permute-start | bytes 2064392 | tf_op jit(solution)/shard_map/ppermute | solution.py:13
  273.2 45.5 %copy-start.12 = (bf16[192,3584]{1,0:T(8,128)(2,1)}, bf16[192,3584]{1,0:T(8,128)(2,1)S(1)}, u32[]{:S(2)}) copy-start(bf16[192,3584]{1,0:T(8,128)(2,1)S(1)} %maximum_select_fusion.7) | copy-start | bytes 4128772
  273.2 45.5 %copy-start.1 = (bf16[1,3584,512]{2,1,0:T(8,128)(2,1)S(1)}, bf16[1,3584,512]{2,1,0:T(8,128)(2,1)}, u32[]{:S(2)}) copy-start(bf16[1,3584,512]{2,1,0:T(8,128)(2,1)} %param.11) | copy-start | bytes 11010052
  273.2 41.1 %collective-permute-start.7 = (bf16[192,3584]{1,0:T(8,128)(2,1)S(1)}, bf16[192,3584]{1,0:T(8,128)(2,1)S(1)}, u32[]{:S(2)}, u32[]{:S(2)}) collective-permute-start(bf16[192,3584]{1,0:T(8,128)(2,1)S(1)} %maximum_select_fusion.7), channel_id=1, source_target_pairs={{0,16},{8,24},{16,0},{24,8},{1,17},{9,25},{17,1},{25,9},{2,18},{10... | collective-permute-start | bytes 4128776 | tf_op jit(solution)/shard_map/ppermute | solution.py:13
  314.2 4.4 copy-start.21
  318.7 1.7 copy-start.17
  318.7 2.2 copy-start.5
  326.1 33.7 %all-to-all-start.3 = ((bf16[8,12,3584]{2,1,0:T(8,128)(2,1)}), bf16[8,12,3584]{2,1,0:T(8,128)(2,1)S(1)}, u32[]{:S(2)}, u32[]{:S(2)}) async-start(bf16[8,12,3584]{2,1,0:T(8,128)(2,1)} %all_to_all.54), calls=%async_computation.5 | async-start | bytes 1835008 | tf_op jit(solution)/shard_map/all_to_all | solution.py:53
  359.8 11.5 %copy-start.6 = (bf16[8,12,3584]{2,1,0:T(8,128)(2,1)}, bf16[8,12,3584]{2,1,0:T(8,128)(2,1)S(1)}, u32[]{:S(2)}) copy-start(bf16[8,12,3584]{2,1,0:T(8,128)(2,1)S(1)} %all-to-all-done.3) | copy-start | bytes 2064388
  359.8 27.3 %all-to-all-start.1 = ((bf16[8,12,3584]{2,1,0:T(8,128)(2,1)}), bf16[8,12,3584]{2,1,0:T(8,128)(2,1)S(1)}, u32[]{:S(2)}, u32[]{:S(2)}) async-start(bf16[8,12,3584]{2,1,0:T(8,128)(2,1)} %all_to_all.50), calls=%async_computation.2 | async-start | bytes 1835008 | tf_op jit(solution)/shard_map/all_to_all | solution.py:53
  363.4 7.9 %copy-start.16 = (bf16[384,512]{1,0:T(8,128)(2,1)S(1)}, bf16[384,512]{1,0:T(8,128)(2,1)}, u32[]{:S(2)}) copy-start(bf16[384,512]{1,0:T(8,128)(2,1)} %copy-done.15) | copy-start | bytes 1179652
  387.1 11.6 %copy-start.8 = (bf16[8,12,3584]{2,1,0:T(8,128)(2,1)}, bf16[8,12,3584]{2,1,0:T(8,128)(2,1)S(1)}, u32[]{:S(2)}) copy-start(bf16[8,12,3584]{2,1,0:T(8,128)(2,1)S(1)} %all-to-all-done.1) | copy-start | bytes 2064388
  387.1 27.5 %all-to-all-start.5 = ((bf16[8,12,3584]{2,1,0:T(8,128)(2,1)}), bf16[8,12,3584]{2,1,0:T(8,128)(2,1)S(1)}, u32[]{:S(2)}, u32[]{:S(2)}) async-start(bf16[8,12,3584]{2,1,0:T(8,128)(2,1)} %all_to_all.58), calls=%async_computation.8 | async-start | bytes 1835008 | tf_op jit(solution)/shard_map/all_to_all | solution.py:53
  390.9 7.8 %copy-start.14 = (bf16[384,512]{1,0:T(8,128)(2,1)S(1)}, bf16[384,512]{1,0:T(8,128)(2,1)}, u32[]{:S(2)}) copy-start(bf16[384,512]{1,0:T(8,128)(2,1)} %copy-done.13) | copy-start | bytes 1179652
  407.3 11.5 %copy-start.24 = (bf16[384,512]{1,0:T(8,128)(2,1)S(1)}, bf16[384,512]{1,0:T(8,128)(2,1)}, u32[]{:S(2)}) copy-start(bf16[384,512]{1,0:T(8,128)(2,1)} %copy-done.23) | copy-start | bytes 1179652
  414.6 4.2 copy-start.10
  414.6 28.0 %all-to-all-start.7 = ((bf16[8,12,3584]{2,1,0:T(8,128)(2,1)}), bf16[8,12,3584]{2,1,0:T(8,128)(2,1)}, u32[]{:S(2)}, u32[]{:S(2)}) async-start(bf16[8,12,3584]{2,1,0:T(8,128)(2,1)} %all_to_all.62), calls=%async_computation.11 | async-start | bytes 1835008 | tf_op jit(solution)/shard_map/all_to_all | solution.py:53
  418.8 8.9 %copy-start.7 = (bf16[8,12,3584]{2,1,0:T(8,128)(2,1)S(1)}, bf16[8,12,3584]{2,1,0:T(8,128)(2,1)}, u32[]{:S(2)}) copy-start(bf16[8,12,3584]{2,1,0:T(8,128)(2,1)} %copy-done.6) | copy-start | bytes 2064388
  418.8 8.8 %copy-start.9 = (bf16[8,12,3584]{2,1,0:T(8,128)(2,1)S(1)}, bf16[8,12,3584]{2,1,0:T(8,128)(2,1)}, u32[]{:S(2)}) copy-start(bf16[8,12,3584]{2,1,0:T(8,128)(2,1)} %copy-done.8) | copy-start | bytes 2064388
Sparse Core Ops, SparseCore 0:
  111.8 55.0 reduce-scatter.6
  187.8 56.0 reduce-scatter.4
  258.5 55.7 reduce-scatter.8
  324.1 45.2 reduce-scatter.10
